TPU v7x, 256 devices: a whole 4x4x8 slice. The times are simulated.
256 devices in a mesh: dp: 32 (over z, x), mp: 8 (over y, core).
Axes of the slice: x: 4, y: 4, z: 8, core: 2. Of those that a mesh axis runs over, the one named last changes fastest.
Arguments:
- token_ids: int32 [2048, 7], replicated, may hold values from 0 to 65535
- lengths: int32 [2048], replicated, may hold values from 1 to 7, as said below
- pack_dest: int32 [2048], replicated, may hold values from 0 to 31, as said below
- ref_hidden: bfloat16 [2048, 7, 4096], P('dp', None, 'mp'), may hold values from -45 to 45
- reward_hidden: bfloat16 [2048, 7, 4096], P('dp', None, 'mp'), may hold values from -140 to 140
- head_weight: bfloat16 [4096, 65536], P('mp', 'dp'), may hold values from -0.25 to 0.25
- norm_gain: float32 [4096], P('mp'), may hold values from 0.1 to 1.9
- score_weight: float32 [4096], P('mp'), may hold values from -0.09375 to 0.09375
- value_weight: float32 [4096], P('mp'), may hold values from -0.09375 to 0.09375
- old_logprob: float32 [8192], P('dp'), may hold values from -14 to -1
Outputs:
- ref_logprob: float32 [8192], P('dp')
- advantage: float32 [8192], P('dp')
Inputs may be any that keep to these rules, and one draw needn't show every extreme that they name: `pack_dest`: request i belongs to request shard i // 64. Each request shard sends exactly 2 of its requests to every packed shard. A packed shard lists its requests by request shard, then by request index, and packs their tokens in that order from slot 0. In that order the requests of a packed shard form pairs whose lengths sum to 8, so every packed shard holds exactly 256 tokens; every packed shard has a request of length 1 and one of length 7.
All inputs are finite; a program needn't handle non-finite values.
Results may differ from a plain program's by a relative error of at most 0.0003.
Values may be sent and summed in bfloat16 or wider, within the bound.
No kernel may reach another device: no remote copies, remote signals or barrier semaphores. Data moves between devices by JAX's collectives and lax.ppermute only.
A program may use at most 192 MiB of HBM per device.

v0:
```python
import jax
import jax.numpy as jnp
from jax import lax
from jax.sharding import PartitionSpec as P

kl_coef = 0.1
discount = 0.99
gae_mix = 0.95
norm_eps = 1e-05


def pair_rank(dest):
    count = dest.shape[-1]
    idx = jnp.arange(count, dtype=jnp.int32)
    same = dest[..., None, :] == dest[..., :, None]
    earlier = idx[None, :] < idx[:, None]
    return jnp.sum(jnp.logical_and(same, earlier).astype(jnp.int32), axis=-1)


def body(
    token_ids,
    lengths,
    pack_dest,
    ref_hidden,
    reward_hidden,
    head_weight,
    norm_gain,
    score_weight,
    value_weight,
    old_logprob,
):
    shards = lax.axis_size("dp")
    ways = lax.axis_size("mp")
    me = lax.axis_index("dp")
    part = lax.axis_index("mp")
    req_dev, max_len, width_dev = ref_hidden.shape
    pair_len = max_len + 1
    slot_dev = shards * pair_len
    sub_len = slot_dev // ways
    blocks = sub_len // pair_len
    width_full = width_dev * ways
    steps = jnp.arange(max_len, dtype=jnp.int32)
    dest = lax.dynamic_slice_in_dim(pack_dest, me * req_dev, req_dev)
    size = lax.dynamic_slice_in_dim(lengths, me * req_dev, req_dev)
    rank = pair_rank(dest)
    row = dest[:, None] * pair_len + steps[None, :] + rank[:, None] * (pair_len - size[:, None])
    row = jnp.where(steps[None, :] < size[:, None], row, -1).reshape(-1)
    onehot = (row[None, :] == jnp.arange(slot_dev, dtype=jnp.int32)[:, None]).astype(jnp.bfloat16)
    ref_send = jnp.dot(
        onehot, ref_hidden.reshape(req_dev * max_len, width_dev), preferred_element_type=jnp.float32
    ).astype(jnp.bfloat16)
    reward_send = jnp.dot(
        onehot,
        reward_hidden.reshape(req_dev * max_len, width_dev),
        preferred_element_type=jnp.float32,
    ).astype(jnp.bfloat16)
    send = jnp.concatenate([ref_send, reward_send], axis=1).reshape(shards, pair_len, 2 * width_dev)
    got = lax.all_to_all(send, "dp", 0, 0, tiled=True).reshape(slot_dev, 2 * width_dev)
    ref_packed = got[:, :width_dev]
    reward_packed = got[:, width_dev:]
    own_rows = lax.all_to_all(
        ref_packed.reshape(ways, sub_len, width_dev), "mp", 0, 2, tiled=True
    ).reshape(sub_len, width_full)
    block_rows = lax.all_gather(own_rows, "dp", axis=0, tiled=True)
    weight = lax.all_gather(head_weight, "mp", axis=0, tiled=True)
    first_src = part * blocks
    dest4 = lax.dynamic_slice_in_dim(pack_dest, first_src * req_dev, blocks * req_dev).reshape(
        blocks, req_dev
    )
    size4 = lax.dynamic_slice_in_dim(lengths, first_src * req_dev, blocks * req_dev).reshape(
        blocks, req_dev
    )
    tok4 = lax.dynamic_slice_in_dim(token_ids, first_src * req_dev, blocks * req_dev, axis=0)
    rank4 = pair_rank(dest4)
    key = (
        dest4[:, :, None] * sub_len
        + jnp.arange(blocks, dtype=jnp.int32)[:, None, None] * pair_len
        + steps[None, None, :]
        + rank4[:, :, None] * (pair_len - size4[:, :, None])
    )
    key = jnp.where(steps[None, None, :] < size4[:, :, None], key, -1).reshape(-1)
    hits = key[None, :] == jnp.arange(shards * sub_len, dtype=jnp.int32)[:, None]
    targets = jnp.sum(jnp.where(hits, tok4.reshape(-1)[None, :], 0), axis=1)
    logits = jnp.dot(block_rows, weight, preferred_element_type=jnp.float32)
    vocab_dev = head_weight.shape[1]
    row_max = jnp.max(logits, axis=1)
    exp_total = jnp.sum(jnp.exp(logits - row_max[:, None]), axis=1)
    column = jnp.arange(vocab_dev, dtype=jnp.int32)[None, :] + me * vocab_dev
    target_logit = jnp.sum(jnp.where(column == targets[:, None], logits, 0.0), axis=1)
    stats = jnp.stack([row_max, exp_total, target_logit]).reshape(3, shards, sub_len)
    stats = lax.all_to_all(stats, "dp", 1, 1, tiled=True)
    joint_max = jnp.max(stats[0], axis=0)
    joint_total = jnp.sum(stats[1] * jnp.exp(stats[0] - joint_max[None, :]), axis=0)
    joint_target = jnp.sum(stats[2], axis=0)
    block_logprob = joint_target - joint_max - jnp.log(joint_total)
    ref_logprob = lax.all_gather(block_logprob, "mp", axis=0, tiled=True)
    hidden_f = reward_packed.astype(jnp.float32)
    sums = jnp.stack(
        [
            jnp.sum(hidden_f * hidden_f, axis=1),
            jnp.sum(hidden_f * (norm_gain * score_weight), axis=1),
            jnp.sum(hidden_f * (norm_gain * value_weight), axis=1),
        ]
    )
    squares, score_dot, value_dot = lax.psum(sums, "mp")
    inv_rms = lax.rsqrt(squares / width_full + norm_eps)
    score = score_dot * inv_rms
    value_est = value_dot * inv_rms
    mine = (pack_dest.reshape(shards, req_dev) == me).astype(jnp.int32)
    is_first = jnp.logical_and(mine == 1, jnp.cumsum(mine, axis=1) == 1)
    first_len = jnp.sum(jnp.where(is_first, lengths.reshape(shards, req_dev), 0), axis=1)
    place = jnp.arange(pair_len, dtype=jnp.int32)[None, :]
    is_last = jnp.logical_or(place == first_len[:, None] - 1, place == pair_len - 1)
    is_last_flat = is_last.reshape(-1)
    reward = -kl_coef * (old_logprob - ref_logprob) + jnp.where(is_last_flat, score, 0.0)
    next_value = jnp.concatenate([value_est[1:], jnp.zeros((1,), jnp.float32)])
    not_last = 1.0 - is_last_flat.astype(jnp.float32)
    td_error = (reward + discount * next_value * not_last - value_est).reshape(shards, pair_len)
    decay = discount * gae_mix
    carry = td_error[:, pair_len - 1]
    columns = [carry]
    for step in range(pair_len - 2, -1, -1):
        carry = td_error[:, step] + decay * jnp.where(is_last[:, step], 0.0, carry)
        columns.append(carry)
    advantage = jnp.stack(columns[::-1], axis=1).reshape(-1)
    return (ref_logprob, advantage)


def solution(mesh):
    return jax.shard_map(
        body,
        mesh=mesh,
        in_specs=(
            P(),
            P(),
            P(),
            P("dp", None, "mp"),
            P("dp", None, "mp"),
            P("mp", "dp"),
            P("mp"),
            P("mp"),
            P("mp"),
            P("dp"),
        ),
        out_specs=(P("dp"), P("dp")),
        check_vma=False,
    )
```

profile of v0, /device:TPU:1, one launch (start us, length us, event | category | flops | bytes accessed | tf_op | source)
XLA Modules:
  0.0 304.3 jit_solution(12371459190618607233)
XLA Ops:
  7.3 0.8 broadcast_multiply_fusion
  8.1 0.2 convert_reduce_fusion.1
  8.2 0.8 subtract_multiply_fusion.1
  9.0 0.1 add_select_fusion.1
  9.1 0.1 select_n.99
  9.3 1.3 copy.33
  10.5 0.2 reshape.220
  10.7 1.3 copy.34
  12.0 0.2 reshape.221
  12.2 0.3 convolution_convert_fusion.1
  12.5 0.3 convolution_convert_fusion
  12.9 27.9 %all_to_all.25 = bf16[32,8,1024]{2,1,0:T(8,128)(2,1)S(1)} all-to-all(bf16[32,8,1024]{2,1,0:T(8,128)(2,1)S(1)} %maximum_bitcast_fusion), channel_id=1, replica_groups=mesh['dp'=32,'mp'=8] {'dp'}, dimensions={0} | all-to-all | bytes 1048576 | tf_op jit(solution)/shard_map/all_to_all | solution.py:58
  40.8 13.2 %all_to_all.26 = bf16[8,32,512]{2,1,0:T(8,128)(2,1)S(1)} all-to-all(bf16[8,32,512]{2,1,0:T(8,128)(2,1)S(1)} %bitcast.31), channel_id=1, replica_groups=mesh['dp'=32,'mp'=8] {'mp'}, dimensions={0} | all-to-all | bytes 524288 | tf_op jit(solution)/shard_map/all_to_all | solution.py:61
  54.0 0.7 copy.39
  54.8 0.7 all-gather.5.cloned.1.call-update
  55.5 0.1 dynamic_slice.17
  55.6 0.1 dynamic_slice.18
  55.7 0.1 lt.91
  55.8 0.1 broadcast_in_dim_reshape.2
  56.0 0.2 reduce_window_sum.11
  56.2 0.1 select_reduce_fusion.2
  56.3 0.1 fusion.5
  56.4 0.1 or.14
  56.5 0.1 copy.36
  56.7 0.2 broadcast_in_dim.45
  56.9 0.2 convert_reduce_fusion
  57.2 0.2 add_select_fusion
  57.4 0.2 select_n.102
  57.6 0.6 dynamic-slice
  58.9 0.8 select_reduce_fusion.1
  59.7 0.2 fusion
  59.9 86.8 %all-gather.3.cloned.1.call-done = bf16[1024,4096]{1,0:T(8,128)(2,1)} async-done(((bf16[32,4096]{1,0:T(8,128)(2,1)}), bf16[1024,4096]{1,0:T(8,128)(2,1)}) %all-gather.3.cloned.1.call-update) | async-done | bytes 8388624 | tf_op jit(solution)/shard_map/all_gather | solution.py:64
  146.7 87.6 %all-gather.5.cloned.1.call-done = bf16[4096,2048]{1,0:T(8,128)(2,1)} async-done(((bf16[512,2048]{1,0:T(8,128)(2,1)}), bf16[4096,2048]{1,0:T(8,128)(2,1)}) %all-gather.5.cloned.1.call-update) | async-done | bytes 16777232 | tf_op jit(solution)/shard_map/all_gather | solution.py:65
  234.3 24.2 %fusion.12 = (f32[1024]{0:T(1024)S(1)}, f32[1024,2048]{1,0:T(8,128)}) fusion(bf16[1024,4096]{1,0:T(8,128)(2,1)} %all-gather.3.cloned.1.call-done, bf16[4096,2048]{1,0:T(8,128)(2,1)} %all-gather.5.cloned.1.call-done), kind=kOutput, calls=%fused_computation.58 | convolution fusion | flops 17181966336 | bytes 33558528 | tf_op jit(solution)/shard_map/dot_general | solution.py:84
  258.5 0.1 stack.34
  258.6 4.7 %exponential_reduce_fusion = (f32[1024]{0:T(1024)S(1)}, f32[1024]{0:T(1024)S(1)}) fusion(f32[1024,2048]{1,0:T(8,128)} %get-tuple-element.29, f32[1024]{0:T(1024)S(1)} %get-tuple-element.28, s32[1024]{0:T(1024)S(1)} %select_reduce_fusion.1, s32[2048]{0:T(1024)S(1)} %iota_add_fusion), kind=kLoop, calls=%fused_computation.1 | loop fusion | flops 10483712 | bytes 8413184 | tf_op jit(solution)/shard_map/reduce_sum | solution.py:87
  263.2 0.1 stack.35
  263.3 0.1 stack.36
  263.4 0.7 pad_maximum_fusion
  264.1 9.5 %all-to-all-start.2 = ((f32[3,32,32]{2,0,1:T(4,128)}), f32[3,32,32]{2,0,1:T(4,128)S(1)}, u32[]{:S(2)}, u32[]{:S(2)}) async-start(f32[3,32,32]{2,0,1:T(4,128)} %pad_maximum_fusion), calls=%async_computation.2 | async-start | bytes 131072 | tf_op jit(solution)/shard_map/all_to_all | solution.py:91
  273.6 8.9 %all-to-all-done.2 = f32[3,32,32]{2,0,1:T(4,128)S(1)} async-done(((f32[3,32,32]{2,0,1:T(4,128)}), f32[3,32,32]{2,0,1:T(4,128)S(1)}, u32[]{:S(2)}, u32[]{:S(2)}) %all-to-all-start.2) | async-done | bytes 12320 | tf_op jit(solution)/shard_map/all_to_all | solution.py:91
  282.6 0.1 subtract_dynamic-update-slice_fusion
  282.7 13.6 %all-reduce.1 = (f32[256]{0:T(256)S(1)}, f32[3,256]{1,0:T(4,128)S(1)}) all-reduce(f32[256]{0:T(256)S(1)} %subtract_dynamic-update-slice_fusion, f32[3,256]{1,0:T(4,128)S(1)} %pad_maximum_fusion.1), channel_id=1, replica_groups=mesh['dp'=32,'mp'=8] {'mp'}, use_global_device_ids=true, to_apply=%add | all-reduce | flops 1024 | bytes 8192
  296.4 0.1 fusion.10
  296.5 0.1 reshape.227
  296.6 0.1 slice_add_fusion.6
  296.7 0.1 stack.42
  296.8 0.7 reshape.228
  (41 shorter events, 0.7 us)
Async XLA Ops:
  7.2 49.3 %copy-start = (s32[2048,7]{0,1:T(8,128)S(1)}, s32[2048,7]{0,1:T(8,128)}, u32[]{:S(2)}) copy-start(s32[2048,7]{0,1:T(8,128)} %param.10) | copy-start | bytes 172036
  7.2 50.4 %copy-start.8 = (u32[256]{0:T(256)S(1)}, u32[256]{0:T(256)}, u32[]{:S(2)}) copy-start(u32[256]{0:T(256)} %constant.56) | copy-start | bytes 3076
  7.2 48.4 %copy-start.2 = (s32[2048]{0:T(1024)S(1)}, s32[2048]{0:T(1024)}, u32[]{:S(2)}) copy-start(s32[2048]{0:T(1024)} %param.12) | copy-start | bytes 24580
  7.2 48.3 %copy-start.1 = (s32[2048]{0:T(1024)S(1)}, s32[2048]{0:T(1024)}, u32[]{:S(2)}) copy-start(s32[2048]{0:T(1024)} %param.11) | copy-start | bytes 24580
  7.2 51.6 %copy-start.5 = (f32[512]{0:T(512)S(1)}, f32[512]{0:T(512)}, u32[]{:S(2)}) copy-start(f32[512]{0:T(512)} %param.18) | copy-start | bytes 6148
  7.2 51.6 %copy-start.4 = (f32[512]{0:T(512)S(1)}, f32[512]{0:T(512)}, u32[]{:S(2)}) copy-start(f32[512]{0:T(512)} %param.17) | copy-start | bytes 6148
  7.2 51.6 %copy-start.3 = (f32[512]{0:T(512)S(1)}, f32[512]{0:T(512)}, u32[]{:S(2)}) copy-start(f32[512]{0:T(512)} %param.16) | copy-start | bytes 6148
  7.2 139.5 %all-gather.3.cloned.1.call-start = ((), (), s32[]{:S(2)}) async-start(), calls=%async_computation.3 | async-start | bytes 8650752 | tf_op jit(solution)/shard_map/all_gather | solution.py:64
  54.7 179.6 %all-gather.5.cloned.1.call-start = ((), (), s32[]{:S(2)}) async-start(), calls=%async_computation.4 | async-start | bytes 18874368 | tf_op jit(solution)/shard_map/all_gather | solution.py:65
  258.5 37.9 %copy-start.6 = (f32[256]{0:T(256)S(1)}, f32[256]{0:T(256)}, u32[]{:S(2)}) copy-start(f32[256]{0:T(256)} %param.19) | copy-start | bytes 3076
  264.1 18.4 %all-to-all-start.2 = ((f32[3,32,32]{2,0,1:T(4,128)}), f32[3,32,32]{2,0,1:T(4,128)S(1)}, u32[]{:S(2)}, u32[]{:S(2)}) async-start(f32[3,32,32]{2,0,1:T(4,128)} %pad_maximum_fusion), calls=%async_computation.2 | async-start | bytes 131072 | tf_op jit(solution)/shard_map/all_to_all | solution.py:91
  296.3 1.2 copy-start.7
Sparse Core Ops, SparseCore 0:
  54.8 91.8 all-gather.2
  148.6 85.6 all-gather.4
where the time goes:
time: 305 us; the launch traced here: 304 us
  waiting for transfers between devices  184 us (60%)
  blocking collectives  54.7 us (18%)
  matrix products  24.8 us (8%)
  between operations  15 us (5%)
  starting transfers between devices  9.61 us (3%)
  other arithmetic  9.59 us (3%)
  local copies, waits for them, and re-layouts  6.68 us (2%)
    all_gather x1, waiting for transfers between devices, body(): weight = lax.all_gather(head_weight, 'mp', axis=0, tiled=True)  87.6 us
    all_gather x1, waiting for transfers between devices, body(): block_rows = lax.all_gather(own_rows, 'dp', axis=0, tiled=True)  86.8 us
    all_to_all x1, blocking collectives, body(): lax.all_to_all(send, 'dp', 0, 0, tiled=True)  27.9 us
    dot_general x1, matrix products, body(): logits = jnp.dot(block_rows, weight, preferred_element_type=jnp.float32)  24.2 us
    unnamed x1, blocking collectives  13.6 us
    all_to_all x1, blocking collectives, body(): lax.all_to_all(ref_packed.reshape(ways, sub_len, width_dev), 'mp', 0, 2,...  13.2 us
    all_to_all x1, starting transfers between devices, body(): stats = lax.all_to_all(stats, 'dp', 1, 1, tiled=True)  9.53 us
    all_to_all x1, waiting for transfers between devices, body(): stats = lax.all_to_all(stats, 'dp', 1, 1, tiled=True)  8.86 us
  transfers between devices with their start and end apart: 3, of which 3 were waited for; matrix products, arithmetic and copies ran while one was open for 1% of the time, Pallas kernels for 0%

commit v1 on v0

--- a/solution.py
+++ b/solution.py
@@ -62,7 +62,9 @@
         ref_packed.reshape(ways, sub_len, width_dev), "mp", 0, 2, tiled=True
     ).reshape(sub_len, width_full)
     block_rows = lax.all_gather(own_rows, "dp", axis=0, tiled=True)
-    weight = lax.all_gather(head_weight, "mp", axis=0, tiled=True)
+    weight = jnp.concatenate(
+        lax.all_to_all(jnp.stack([head_weight] * lax.axis_size("mp")), "mp", 0, 0), axis=0
+    )
     first_src = part * blocks
     dest4 = lax.dynamic_slice_in_dim(pack_dest, first_src * req_dev, blocks * req_dev).reshape(
         blocks, req_dev

time: 305 us -> 319 us (1.046)
  local copies, waits for them, and re-layouts: 6.68 us -> 13.4 us
  waiting for transfers between devices: 184 us -> 188 us
    all_to_all x0 -> x1, waiting for transfers between devices: none -> 179 us  [body(): lax.all_to_all(jnp.stack([head_weight] * lax.axis_size('mp')), 'mp', 0, 0)]
    all_gather x1 -> x0, waiting for transfers between devices: 87.6 us -> none  [body(): weight = lax.all_gather(head_weight, 'mp', axis=0, tiled=True)]
    all_gather x1, waiting for transfers between devices: 86.8 us -> 0.01 us  [body(): block_rows = lax.all_gather(own_rows, 'dp', axis=0, tiled=True)]
    all_to_all x0 -> x1, starting transfers between devices: none -> 6.81 us  [body(): lax.all_to_all(jnp.stack([head_weight] * lax.axis_size('mp')), 'mp', 0, 0)]
    another operation x0 -> x1, local copies, waits for them, and re-layouts: none -> 5.98 us  [body(): jnp.stack([head_weight] * lax.axis_size('mp'))]
    all_to_all x1, starting transfers between devices: 9.53 us -> 4.35 us  [body(): stats = lax.all_to_all(stats, 'dp', 1, 1, tiled=True)]
  transfers between devices with their start and end apart: 3 -> 3, of which waited for: 3 -> 2; matrix products, arithmetic and copies ran while one was open for 1% -> 3% of each run, Pallas kernels for 0% -> 0%
where the time goes in v1:
time: 319 us
  waiting for transfers between devices  188 us (59%)
  blocking collectives  55.4 us (17%)
  matrix products  25.9 us (8%)
  between operations  15 us (5%)
  local copies, waits for them, and re-layouts  13.4 us (4%)
  starting transfers between devices  11.2 us (4%)
  other arithmetic  9.72 us (3%)
    all_to_all x1, waiting for transfers between devices, body(): lax.all_to_all(jnp.stack([head_weight] * lax.axis_size('mp')), 'mp', 0, 0)  179 us
    all_to_all x1, blocking collectives, body(): lax.all_to_all(send, 'dp', 0, 0, tiled=True)  27.9 us
    dot_general x1, matrix products, body(): logits = jnp.dot(block_rows, weight, preferred_element_type=jnp.float32)  24.2 us
    unnamed x1, blocking collectives  14.3 us
    all_to_all x1, blocking collectives, body(): lax.all_to_all(ref_packed.reshape(ways, sub_len, width_dev), 'mp', 0, 2,...  13.2 us
    all_to_all x1, waiting for transfers between devices, body(): stats = lax.all_to_all(stats, 'dp', 1, 1, tiled=True)  8.82 us
    all_to_all x1, starting transfers between devices, body(): lax.all_to_all(jnp.stack([head_weight] * lax.axis_size('mp')), 'mp', 0, 0)  6.81 us
  transfers between devices with their start and end apart: 3, of which 2 were waited for; matrix products, arithmetic and copies ran while one was open for 3% of the time, Pallas kernels for 0%

profile of v1, /device:TPU:1, one launch (start us, length us, event | category | flops | bytes accessed | tf_op | source)
XLA Modules:
  0.0 318.6 jit_solution(14062374751175661631)
XLA Ops:
  7.2 0.9 broadcast_multiply_fusion
  8.1 0.2 convert_reduce_fusion.1
  8.3 0.8 subtract_multiply_fusion.1
  9.1 0.1 add_select_fusion.1
  9.2 0.1 select_n.99
  9.3 1.3 copy.33
  10.6 0.2 reshape.225
  10.8 1.3 copy.34
  12.1 0.9 reshape.226
  13.0 0.3 convolution_convert_fusion.1
  13.3 1.3 convolution_convert_fusion
  14.7 27.9 %all_to_all.30 = bf16[32,8,1024]{2,1,0:T(8,128)(2,1)S(1)} all-to-all(bf16[32,8,1024]{2,1,0:T(8,128)(2,1)S(1)} %maximum_bitcast_fusion), channel_id=1, replica_groups=mesh['dp'=32,'mp'=8] {'dp'}, dimensions={0} | all-to-all | bytes 1048576 | tf_op jit(solution)/shard_map/all_to_all | solution.py:58
  42.7 13.2 %all_to_all.31 = bf16[8,32,512]{2,1,0:T(8,128)(2,1)S(1)} all-to-all(bf16[8,32,512]{2,1,0:T(8,128)(2,1)S(1)} %bitcast.32), channel_id=1, replica_groups=mesh['dp'=32,'mp'=8] {'mp'}, dimensions={0} | all-to-all | bytes 524288 | tf_op jit(solution)/shard_map/all_to_all | solution.py:61
  55.8 0.7 copy.39
  56.6 6.0 %stack.20 = bf16[8,512,2048]{2,1,0:T(8,128)(2,1)} broadcast(bf16[512,2048]{1,0:T(8,128)(2,1)S(1)} %copy-done.1), dimensions={1,2} | broadcast | bytes 18874368 | tf_op jit(solution)/shard_map/stack | solution.py:66
  62.6 6.8 %all-to-all-start.2 = ((bf16[8,512,2048]{2,1,0:T(8,128)(2,1)}), bf16[8,512,2048]{2,1,0:T(8,128)(2,1)}, u32[]{:S(2)}, u32[]{:S(2)}) async-start(bf16[8,512,2048]{2,1,0:T(8,128)(2,1)} %stack.20), calls=%async_computation.2 | async-start | bytes 33554432 | tf_op jit(solution)/shard_map/all_to_all | solution.py:66
  69.4 0.1 dynamic_slice.17
  69.5 0.1 dynamic_slice.18
  69.6 0.1 lt.91
  69.7 0.1 broadcast_in_dim_reshape.2
  69.9 0.2 reduce_window_sum.11
  70.1 0.1 select_reduce_fusion.2
  70.2 0.1 fusion.5
  70.3 0.1 or.14
  70.5 0.1 copy.36
  70.6 0.2 broadcast_in_dim.45
  70.8 0.2 convert_reduce_fusion
  71.1 0.2 add_select_fusion
  71.3 0.2 select_n.102
  71.5 0.6 dynamic-slice
  72.8 0.8 select_reduce_fusion.1
  73.6 0.2 fusion
  73.8 179.2 %all-to-all-done.2 = bf16[8,512,2048]{2,1,0:T(8,128)(2,1)} async-done(((bf16[8,512,2048]{2,1,0:T(8,128)(2,1)}), bf16[8,512,2048]{2,1,0:T(8,128)(2,1)}, u32[]{:S(2)}, u32[]{:S(2)}) %all-to-all-start.2) | async-done | bytes 16777248 | tf_op jit(solution)/shard_map/all_to_all | solution.py:66
  253.1 24.2 %fusion.12 = (f32[1024]{0:T(1024)S(1)}, f32[1024,2048]{1,0:T(8,128)}) fusion(bf16[1024,4096]{1,0:T(8,128)(2,1)} %all-gather.2.cloned.1.call-done, bf16[4096,2048]{1,0:T(8,128)(2,1)} %bitcast.5), kind=kOutput, calls=%fused_computation.58 | convolution fusion | flops 17181966336 | bytes 33558528 | tf_op jit(solution)/shard_map/dot_general | solution.py:86
  277.3 0.1 stack.21
  277.4 4.6 %exponential_reduce_fusion = (f32[1024]{0:T(1024)S(1)}, f32[1024]{0:T(1024)S(1)}) fusion(f32[1024,2048]{1,0:T(8,128)} %get-tuple-element.29, f32[1024]{0:T(1024)S(1)} %get-tuple-element.28, s32[1024]{0:T(1024)S(1)} %select_reduce_fusion.1, s32[2048]{0:T(1024)S(1)} %iota_add_fusion), kind=kLoop, calls=%fused_computation.1 | loop fusion | flops 10483712 | bytes 8413184 | tf_op jit(solution)/shard_map/reduce_sum | solution.py:89
  282.0 0.1 stack.22
  282.1 0.1 stack.23
  282.2 0.7 pad_maximum_fusion
  282.9 4.3 %all-to-all-start.3 = ((f32[3,32,32]{2,0,1:T(4,128)}), f32[3,32,32]{2,0,1:T(4,128)S(1)}, u32[]{:S(2)}, u32[]{:S(2)}) async-start(f32[3,32,32]{2,0,1:T(4,128)} %pad_maximum_fusion), calls=%async_computation.3 | async-start | bytes 131072 | tf_op jit(solution)/shard_map/all_to_all | solution.py:93
  287.2 8.8 %all-to-all-done.3 = f32[3,32,32]{2,0,1:T(4,128)S(1)} async-done(((f32[3,32,32]{2,0,1:T(4,128)}), f32[3,32,32]{2,0,1:T(4,128)S(1)}, u32[]{:S(2)}, u32[]{:S(2)}) %all-to-all-start.3) | async-done | bytes 12320 | tf_op jit(solution)/shard_map/all_to_all | solution.py:93
  296.2 0.1 subtract_dynamic-update-slice_fusion
  296.3 14.3 %all-reduce.1 = (f32[256]{0:T(256)S(1)}, f32[3,256]{1,0:T(4,128)S(1)}) all-reduce(f32[256]{0:T(256)S(1)} %subtract_dynamic-update-slice_fusion, f32[3,256]{1,0:T(4,128)S(1)} %pad_maximum_fusion.1), channel_id=1, replica_groups=mesh['dp'=32,'mp'=8] {'mp'}, use_global_device_ids=true, to_apply=%add | all-reduce | flops 1024 | bytes 8192
  310.7 0.1 fusion.10
  310.8 0.1 reshape.233
  310.9 0.1 slice_add_fusion.6
  311.0 0.1 stack.54
  311.1 0.7 reshape.234
  (43 shorter events, 0.7 us)
Async XLA Ops:
  7.2 63.3 %copy-start = (s32[2048,7]{0,1:T(8,128)S(1)}, s32[2048,7]{0,1:T(8,128)}, u32[]{:S(2)}) copy-start(s32[2048,7]{0,1:T(8,128)} %param.10) | copy-start | bytes 172036
  7.2 49.4 %copy-start.1 = (bf16[512,2048]{1,0:T(8,128)(2,1)S(1)}, bf16[512,2048]{1,0:T(8,128)(2,1)}, u32[]{:S(2)}) copy-start(bf16[512,2048]{1,0:T(8,128)(2,1)} %param.15) | copy-start | bytes 6291460
  7.2 245.9 %all-gather.2.cloned.1.call-start = ((), (), s32[]{:S(2)}) async-start(), calls=%async_computation.4 | async-start | bytes 8650752 | tf_op jit(solution)/shard_map/all_gather | solution.py:64
  62.6 6.9 %copy-start.2 = (s32[2048]{0:T(1024)S(1)}, s32[2048]{0:T(1024)}, u32[]{:S(2)}) copy-start(s32[2048]{0:T(1024)} %param.11) | copy-start | bytes 24580
  62.6 6.9 %copy-start.3 = (s32[2048]{0:T(1024)S(1)}, s32[2048]{0:T(1024)}, u32[]{:S(2)}) copy-start(s32[2048]{0:T(1024)} %param.12) | copy-start | bytes 24580
  62.6 9.0 %copy-start.9 = (u32[256]{0:T(256)S(1)}, u32[256]{0:T(256)}, u32[]{:S(2)}) copy-start(u32[256]{0:T(256)} %constant.56) | copy-start | bytes 3076
  62.6 10.2 %copy-start.4 = (f32[512]{0:T(512)S(1)}, f32[512]{0:T(512)}, u32[]{:S(2)}) copy-start(f32[512]{0:T(512)} %param.16) | copy-start | bytes 6148
  62.6 10.2 %copy-start.5 = (f32[512]{0:T(512)S(1)}, f32[512]{0:T(512)}, u32[]{:S(2)}) copy-start(f32[512]{0:T(512)} %param.17) | copy-start | bytes 6148
  62.6 10.2 %copy-start.6 = (f32[512]{0:T(512)S(1)}, f32[512]{0:T(512)}, u32[]{:S(2)}) copy-start(f32[512]{0:T(512)} %param.18) | copy-start | bytes 6148
  62.6 190.4 %all-to-all-start.2 = ((bf16[8,512,2048]{2,1,0:T(8,128)(2,1)}), bf16[8,512,2048]{2,1,0:T(8,128)(2,1)}, u32[]{:S(2)}, u32[]{:S(2)}) async-start(bf16[8,512,2048]{2,1,0:T(8,128)(2,1)} %stack.20), calls=%async_computation.2 | async-start | bytes 33554432 | tf_op jit(solution)/shard_map/all_to_all | solution.py:66
  277.3 33.4 %copy-start.7 = (f32[256]{0:T(256)S(1)}, f32[256]{0:T(256)}, u32[]{:S(2)}) copy-start(f32[256]{0:T(256)} %param.19) | copy-start | bytes 3076
  282.9 13.2 %all-to-all-start.3 = ((f32[3,32,32]{2,0,1:T(4,128)}), f32[3,32,32]{2,0,1:T(4,128)S(1)}, u32[]{:S(2)}, u32[]{:S(2)}) async-start(f32[3,32,32]{2,0,1:T(4,128)} %pad_maximum_fusion), calls=%async_computation.3 | async-start | bytes 131072 | tf_op jit(solution)/shard_map/all_to_all | solution.py:93
  310.6 1.2 copy-start.8
Sparse Core Ops, SparseCore 0:
  56.7 91.7 all-gather.1
